TPU v7x, 512 devices: a whole 4x8x8 slice. The times are simulated.
512 devices in a mesh: expert: 64 (over z, y), tensor: 8 (over x, core).
Axes of the slice: x: 4, y: 8, z: 8, core: 2. Of those that a mesh axis runs over, the one named last changes fastest.
Arguments:
- hidden_rows: bfloat16 [2, 1024, 3584], P(None, 'expert', 'tensor'), may hold values from -6 to 6
- draft_len: int32 [2, 256], P(None, 'expert'), may hold values from 1 to 4, 640 in all within a row
- expert_ids: int32 [2, 1024, 8], P(None, 'expert'), may hold values from 0 to 55, all different within a row; in each aligned block of 16 rows (0 to 15, 16 to 31, ..., all dimensions but the last counted through in order) at most 4 rows name the same one
- replica: int32 [2, 1024, 8], P(None, 'expert'), may hold values from 0 to 1
- route_gain: float32 [2, 1024, 8], P(None, 'expert'), may hold values from 0.03 to 0.5
- slot_up: bfloat16 [64, 3584, 1024], P('expert', None, 'tensor'), may hold values from -0.09375 to 0.09375
- slot_down: bfloat16 [64, 1024, 3584], P('expert', 'tensor'), may hold values from -0.1875 to 0.1875
- shared_up: bfloat16 [3584, 1024], P(None, 'tensor'), may hold values from -0.09375 to 0.09375
- shared_down: bfloat16 [1024, 3584], P('tensor'), may hold values from -0.1875 to 0.1875
Outputs:
- mixed: bfloat16 [2, 1024, 3584], P(None, 'expert', 'tensor')
Inputs may be any that keep to these rules, and one draw needn't show every extreme that they name: `expert_ids`: in each step, the 16 row places of one index of expert (live or not) name any one expert at most 4 times. Only the first 8 experts have a replica slot; for the other experts the value has no effect. `draft_len`: in each step the lengths of all 256 requests sum to 640.
All inputs are finite; a program needn't handle non-finite values. No bound on the sum of `draft_len` on one device may be relied on, other than what follows from the above.
Results may differ from a plain program's by a relative error of at most 0.019.
Values may be sent and summed in bfloat16 or wider, within the bound.
No kernel may reach another device: no remote copies, remote signals or barrier semaphores. Data moves between devices by JAX's collectives and lax.ppermute only.
A program may use at most 192 MiB of HBM per device.

v0:
```python
import jax
import jax.numpy as jnp
from jax import lax
from jax.sharding import PartitionSpec as P


def route_plan(lengths, chosen, second, gains, slot_count, capacity):
    row_count, top_count = chosen.shape
    span_rows = row_count // lengths.shape[0]
    positions = jnp.arange(row_count, dtype=jnp.int32)
    limit = jnp.repeat(lengths, span_rows, total_repeat_length=row_count)
    live_mask = positions % span_rows < limit
    replicas = slot_count // 8
    experts_all = slot_count - replicas
    slot_index = jnp.where(
        (chosen < replicas) & (second == 1), chosen + experts_all, chosen
    ).reshape(-1)
    valid = jnp.broadcast_to(live_mask[:, None], chosen.shape).reshape(-1)
    onehot = (
        (slot_index[:, None] == jnp.arange(slot_count, dtype=jnp.int32)[None, :]) & valid[:, None]
    ).astype(jnp.int32)
    earlier = jnp.cumsum(onehot, axis=0) - onehot
    order_rank = jnp.sum(earlier * onehot, axis=1)
    target = jnp.where(valid, slot_index * capacity + order_rank, -1)
    buffer_ids = jnp.arange(slot_count * capacity, dtype=jnp.int32)
    picker = jnp.any(
        target.reshape(row_count, top_count)[None, :, :] == buffer_ids[:, None, None], axis=2
    ).astype(jnp.bfloat16)
    weights = (gains * live_mask[:, None].astype(jnp.float32)).reshape(-1)
    return (live_mask, target, picker, weights)


def shards(
    hidden_rows,
    draft_len,
    expert_ids,
    replica,
    route_gain,
    slot_up,
    slot_down,
    shared_up,
    shared_down,
):
    slot_count = lax.axis_size("expert")
    step_count, row_count, _ = hidden_rows.shape
    top_count = expert_ids.shape[2]
    capacity = row_count * top_count // (slot_count - slot_count // 8) + 2
    gathered = lax.all_gather(hidden_rows, "tensor", axis=2, tiled=True)
    width_full = gathered.shape[2]
    plans = [
        route_plan(
            draft_len[index],
            expert_ids[index],
            replica[index],
            route_gain[index],
            slot_count,
            capacity,
        )
        for index in range(step_count)
    ]
    outgoing = []
    for index in range(step_count):
        source = gathered[index]
        packed = jnp.dot(plans[index][2], source, preferred_element_type=jnp.float32).astype(
            jnp.bfloat16
        )
        outgoing.append(packed.reshape(slot_count, capacity, source.shape[1]))
    groups = [[index] for index in range(step_count)]
    returned = [None] * step_count
    for step_group in groups:
        batch = jnp.concatenate([outgoing[index] for index in step_group], axis=1)
        received = lax.all_to_all(batch, "expert", split_axis=0, concat_axis=0, tiled=True)
        flat_rows = received.reshape(-1, width_full)
        hidden = jax.nn.silu(
            jnp.dot(flat_rows, slot_up[0], preferred_element_type=jnp.float32)
        ).astype(jnp.bfloat16)
        partial_value = jnp.dot(hidden, slot_down[0], preferred_element_type=jnp.float32).astype(
            jnp.bfloat16
        )
        partial_value = partial_value.reshape(received.shape[0], -1, width_full)
        answer = lax.all_to_all(partial_value, "expert", split_axis=0, concat_axis=0, tiled=True)
        out_width = answer.shape[2]
        for place, index in enumerate(step_group):
            returned[index] = answer.reshape(-1, out_width)
    routed_terms = []
    shared_terms = []
    for index in range(step_count):
        live_mask, target, picker, weights = plans[index]
        fetched = jnp.take(returned[index], jnp.maximum(target, 0), axis=0).astype(jnp.float32)
        routed = jnp.sum(
            (fetched * weights[:, None]).reshape(row_count, top_count, fetched.shape[1]), axis=1
        )
        shared_act = jax.nn.silu(
            jnp.dot(gathered[index], shared_up, preferred_element_type=jnp.float32)
        ).astype(jnp.bfloat16)
        shared_out = jnp.dot(shared_act, shared_down, preferred_element_type=jnp.float32)
        routed_terms.append(routed)
        shared_terms.append(shared_out)
    live_all = jnp.stack([plans[index][0] for index in range(step_count)]).astype(jnp.float32)[
        :, :, None
    ]
    terms = (jnp.stack(routed_terms) + jnp.stack(shared_terms)) * live_all
    summed = lax.psum_scatter(terms.astype(jnp.bfloat16), "tensor", scatter_dimension=2, tiled=True)
    return summed


def solution(mesh):
    return jax.shard_map(
        shards,
        mesh=mesh,
        in_specs=(
            P(None, "expert", "tensor"),
            P(None, "expert"),
            P(None, "expert", None),
            P(None, "expert", None),
            P(None, "expert", None),
            P("expert", None, "tensor"),
            P("expert", "tensor", None),
            P(None, "tensor"),
            P("tensor", None),
        ),
        out_specs=P(None, "expert", "tensor"),
        check_vma=False,
    )
```

profile of v0, /device:TPU:8, one launch (start us, length us, event | category | flops | bytes accessed | tf_op | source)
XLA Modules:
  0.0 314.1 jit_solution(14471994504677403090)
XLA Ops:
  6.5 0.8 slice_bitcast_fusion.1
  7.3 0.7 pad_clamp_fusion.2
  8.0 0.7 gather_fusion.2
  8.6 0.7 gather_fusion
  9.4 0.1 and.64
  9.5 0.7 fusion.61
  10.3 0.1 squeeze.37
  10.4 0.7 fusion.60
  11.2 0.1 eq.84
  11.3 0.1 fusion.27
  11.4 0.2 reduce_window_sum.31
  11.6 0.2 select_reduce_fusion.1
  11.7 0.1 reduce_sum.41
  11.8 0.1 fusion.33
  11.9 0.1 fusion.16
  12.0 0.9 copy.58
  13.0 15.1 %all_gather.3 = bf16[2,16,3584]{1,0,2:T(2,128)(2,1)S(1)} all-gather(bf16[2,16,448]{1,0,2:T(2,128)(2,1)S(1)} %copy.58), channel_id=1, replica_groups=mesh['expert'=64,'tensor'=8] {'tensor'}, dimensions={2}, use_global_device_ids=true | all-gather | bytes 258048 | tf_op jit(solution)/shard_map/all_gather | solution.py:48
  28.1 3.5 %fusion.58 = (bf16[1,16,3584]{1,0,2:T(2,128)(2,1)S(1)}, bf16[1,16,3584]{1,0,2:T(2,128)(2,1)}) fusion(bf16[2,16,3584]{1,0,2:T(2,128)(2,1)S(1)} %all_gather.3), kind=kLoop, calls=%fused_computation.82 | loop fusion | bytes 458752 | tf_op jit(solution)/shard_map/slice | solution.py:63
  31.6 1.8 copy.73
  33.3 0.7 convolution_convert_fusion.3
  34.0 1.5 reshape.191
  35.5 16.6 %all-to-all-start = ((bf16[64,4,3584]{2,1,0:T(4,128)(2,1)}), bf16[64,4,3584]{2,1,0:T(4,128)(2,1)S(1)}, u32[]{:S(2)}, u32[]{:S(2)}) async-start(bf16[64,4,3584]{2,1,0:T(4,128)(2,1)} %reshape.191), calls=%async_computation | async-start | bytes 3670016 | tf_op jit(solution)/shard_map/all_to_all | solution.py:72
  52.2 0.1 and.69
  52.3 0.1 squeeze.43
  52.5 0.1 eq.93
  52.6 0.1 fusion.29
  52.7 0.2 reduce_window_sum.32
  52.9 0.2 select_reduce_fusion
  53.2 3.5 %copy.76 = bf16[1,16,3584]{2,1,0:T(8,128)(2,1)S(1)} copy(bf16[1,16,3584]{1,0,2:T(2,128)(2,1)} %get-tuple-element.32) | data formatting | bytes 229376
  56.8 0.1 fusion.17
  56.9 1.9 convolution_convert_fusion.2
  58.8 4.1 %reshape.196 = bf16[64,4,3584]{2,1,0:T(4,128)(2,1)} reshape(bf16[256,3584]{1,0:T(8,128)(2,1)} %convolution_convert_fusion.2) | data formatting | bytes 3670016 | tf_op jit(solution)/shard_map/reshape | solution.py:67
  62.9 36.4 %all-to-all-done = bf16[64,4,3584]{2,1,0:T(4,128)(2,1)S(1)} async-done(((bf16[64,4,3584]{2,1,0:T(4,128)(2,1)}), bf16[64,4,3584]{2,1,0:T(4,128)(2,1)S(1)}, u32[]{:S(2)}, u32[]{:S(2)}) %all-to-all-start) | async-done | bytes 1835040 | tf_op jit(solution)/shard_map/all_to_all | solution.py:72
  99.3 8.4 %all-to-all-start.2 = ((bf16[64,4,3584]{2,1,0:T(4,128)(2,1)}), bf16[64,4,3584]{2,1,0:T(4,128)(2,1)}, u32[]{:S(2)}, u32[]{:S(2)}) async-start(bf16[64,4,3584]{2,1,0:T(4,128)(2,1)} %reshape.196), calls=%async_computation.2 | async-start | bytes 3670016 | tf_op jit(solution)/shard_map/all_to_all | solution.py:72
  107.7 1.5 reshape.192
  109.2 2.9 convolution_convert_fusion.1
  112.1 1.5 reshape.193
  113.6 40.3 %all-to-all-done.2 = bf16[64,4,3584]{2,1,0:T(4,128)(2,1)} async-done(((bf16[64,4,3584]{2,1,0:T(4,128)(2,1)}), bf16[64,4,3584]{2,1,0:T(4,128)(2,1)}, u32[]{:S(2)}, u32[]{:S(2)}) %all-to-all-start.2) | async-done | bytes 1835040 | tf_op jit(solution)/shard_map/all_to_all | solution.py:72
  153.9 7.5 %all-to-all-start.1 = ((bf16[64,4,3584]{2,1,0:T(4,128)(2,1)}), bf16[64,4,3584]{2,1,0:T(4,128)(2,1)S(1)}, u32[]{:S(2)}, u32[]{:S(2)}) async-start(bf16[64,4,3584]{2,1,0:T(4,128)(2,1)} %reshape.193), calls=%async_computation.1 | async-start | bytes 3670016 | tf_op jit(solution)/shard_map/all_to_all | solution.py:81
  161.5 3.9 %reshape.197 = bf16[256,3584]{1,0:T(8,128)(2,1)} reshape(bf16[64,4,3584]{2,1,0:T(4,128)(2,1)} %all-to-all-done.2) | data formatting | bytes 3670016 | tf_op jit(solution)/shard_map/reshape | solution.py:73
  165.4 4.2 %convolution_convert_fusion = bf16[256,3584]{1,0:T(8,128)(2,1)} fusion(bf16[1,128,3584]{2,1,0:T(8,128)(2,1)S(1)} %copy-done, bf16[256,3584]{1,0:T(8,128)(2,1)} %reshape.197, bf16[1,3584,128]{2,1,0:T(8,128)(2,1)} %param.22), kind=kOutput, calls=%fused_computation.4 | convolution fusion | flops 470843392 | bytes 5505024 | tf_op jit(solution)/shard_map/dot_general | solution.py:77
  169.6 4.1 %reshape.198 = bf16[64,4,3584]{2,1,0:T(4,128)(2,1)} reshape(bf16[256,3584]{1,0:T(8,128)(2,1)} %convolution_convert_fusion) | data formatting | bytes 3670016 | tf_op jit(solution)/shard_map/reshape | solution.py:80
  173.6 33.8 %all-to-all-done.1 = bf16[64,4,3584]{2,1,0:T(4,128)(2,1)S(1)} async-done(((bf16[64,4,3584]{2,1,0:T(4,128)(2,1)}), bf16[64,4,3584]{2,1,0:T(4,128)(2,1)S(1)}, u32[]{:S(2)}, u32[]{:S(2)}) %all-to-all-start.1) | async-done | bytes 1835040 | tf_op jit(solution)/shard_map/all_to_all | solution.py:81
  207.4 1.3 copy-done.1
  208.7 7.3 %all-to-all-start.3 = ((bf16[64,4,3584]{2,1,0:T(4,128)(2,1)}), bf16[64,4,3584]{2,1,0:T(4,128)(2,1)}, u32[]{:S(2)}, u32[]{:S(2)}) async-start(bf16[64,4,3584]{2,1,0:T(4,128)(2,1)} %reshape.198), calls=%async_computation.3 | async-start | bytes 3670016 | tf_op jit(solution)/shard_map/all_to_all | solution.py:81
  216.1 0.1 mul.89
  216.3 0.1 mul.98
  216.5 0.1 squeeze.41
  216.6 0.1 squeeze.45
  216.8 1.9 convolution_bitcast_fusion
  218.7 0.5 convolution_bitcast_fusion.1
  219.2 3.0 reshape.194
  222.2 2.0 gather_fusion.1
  224.2 35.6 %all-to-all-done.3 = bf16[64,4,3584]{2,1,0:T(4,128)(2,1)} async-done(((bf16[64,4,3584]{2,1,0:T(4,128)(2,1)}), bf16[64,4,3584]{2,1,0:T(4,128)(2,1)}, u32[]{:S(2)}, u32[]{:S(2)}) %all-to-all-start.3) | async-done | bytes 1835040 | tf_op jit(solution)/shard_map/all_to_all | solution.py:81
  259.8 2.9 reshape.199
  262.8 2.0 gather_fusion.3
  264.8 1.9 bitcast_reduce_fusion.1
  266.7 1.9 bitcast_reduce_fusion
  268.7 0.1 fusion.7
  268.8 2.4 copy.69
  271.2 1.6 reshape.243
  272.9 32.6 %reduce-scatter.4.cloned.1.call-done = bf16[448,32]{1,0:T(8,128)(2,1)} async-done(((bf16[3584,32]{1,0:T(8,128)(2,1)}), bf16[448,32]{1,0:T(8,128)(2,1)}) %reduce-scatter.4.cloned.1.call-update) | async-done | bytes 28688
  305.5 1.0 reshape.244
  306.5 0.7 copy.70
  (36 shorter events, 1.1 us)
Async XLA Ops:
  6.5 102.7 %copy-start = (bf16[1,128,3584]{2,1,0:T(8,128)(2,1)S(1)}, bf16[1,128,3584]{2,1,0:T(8,128)(2,1)}, u32[]{:S(2)}) copy-start(bf16[1,128,3584]{2,1,0:T(8,128)(2,1)} %param.23) | copy-start | bytes 2752516
  35.5 63.8 %all-to-all-start = ((bf16[64,4,3584]{2,1,0:T(4,128)(2,1)}), bf16[64,4,3584]{2,1,0:T(4,128)(2,1)S(1)}, u32[]{:S(2)}, u32[]{:S(2)}) async-start(bf16[64,4,3584]{2,1,0:T(4,128)(2,1)} %reshape.191), calls=%async_computation | async-start | bytes 3670016 | tf_op jit(solution)/shard_map/all_to_all | solution.py:72
  99.3 54.6 %all-to-all-start.2 = ((bf16[64,4,3584]{2,1,0:T(4,128)(2,1)}), bf16[64,4,3584]{2,1,0:T(4,128)(2,1)}, u32[]{:S(2)}, u32[]{:S(2)}) async-start(bf16[64,4,3584]{2,1,0:T(4,128)(2,1)} %reshape.196), calls=%async_computation.2 | async-start | bytes 3670016 | tf_op jit(solution)/shard_map/all_to_all | solution.py:72
  153.9 53.5 %all-to-all-start.1 = ((bf16[64,4,3584]{2,1,0:T(4,128)(2,1)}), bf16[64,4,3584]{2,1,0:T(4,128)(2,1)S(1)}, u32[]{:S(2)}, u32[]{:S(2)}) async-start(bf16[64,4,3584]{2,1,0:T(4,128)(2,1)} %reshape.193), calls=%async_computation.1 | async-start | bytes 3670016 | tf_op jit(solution)/shard_map/all_to_all | solution.py:81
  173.6 42.8 %copy-start.4 = (f32[2,16,8]{1,2,0:T(8,128)S(1)}, f32[2,16,8]{1,2,0:T(8,128)}, u32[]{:S(2)}) copy-start(f32[2,16,8]{1,2,0:T(8,128)} %param.21) | copy-start | bytes 3076
  207.4 1.3 copy-start.1
  208.7 51.1 %all-to-all-start.3 = ((bf16[64,4,3584]{2,1,0:T(4,128)(2,1)}), bf16[64,4,3584]{2,1,0:T(4,128)(2,1)}, u32[]{:S(2)}, u32[]{:S(2)}) async-start(bf16[64,4,3584]{2,1,0:T(4,128)(2,1)} %reshape.198), calls=%async_computation.3 | async-start | bytes 3670016 | tf_op jit(solution)/shard_map/all_to_all | solution.py:81
  216.0 2.8 copy-start.2
  216.0 2.8 copy-start.3
  216.0 89.5 %reduce-scatter.4.cloned.1.call-start = ((), (), s32[]{:S(2)}) async-start(), calls=%async_computation.5 | async-start | bytes 1032192
Sparse Core Ops, SparseCore 0:
  273.0 32.4 reduce-scatter.3
where the time goes:
time: 315 us; the launch traced here: 314 us
  waiting for transfers between devices  179 us (57%)
  local copies, waits for them, and re-layouts  48.6 us (15%)
  starting transfers between devices  39.8 us (13%)
  blocking collectives  15.1 us (5%)
  between operations  13.7 us (4%)
  matrix products  12.1 us (4%)
  other arithmetic  6 us (2%)
    all_to_all x2, waiting for transfers between devices, shards(): lax.all_to_all(batch, 'expert', split_axis=0, concat_axis=0, tiled=True)  76.8 us
    all_to_all x2, waiting for transfers between devices, shards(): lax.all_to_all(partial_value, 'expert', split_axis=0, concat_axis=0, tile...  69.4 us
    unnamed x2, waiting for transfers between devices  32.7 us
    all_to_all x2, starting transfers between devices, shards(): lax.all_to_all(batch, 'expert', split_axis=0, concat_axis=0, tiled=True)  25 us
    all_gather x1, blocking collectives, shards(): gathered = lax.all_gather(hidden_rows, 'tensor', axis=2, tiled=True)  15.1 us
    all_to_all x2, starting transfers between devices, shards(): lax.all_to_all(partial_value, 'expert', split_axis=0, concat_axis=0, tile...  14.8 us
    unnamed x21, local copies, waits for them, and re-layouts  13.6 us
    dot_general x2, matrix products, shards(): jnp.dot(hidden, slot_down[0], preferred_element_type=jnp.float32)  7.1 us
  transfers between devices with their start and end apart: 5, of which 5 were waited for; matrix products, arithmetic and copies ran while one was open for 12% of the time, Pallas kernels for 0%

commit v1 on v0

--- a/solution.py
+++ b/solution.py
@@ -41,11 +41,23 @@
     shared_up,
     shared_down,
 ):
+
+    def boxes_map(x0, link_axis):
+        return jnp.concatenate(
+            lax.all_to_all(
+                jnp.stack([x0 for _ in range(lax.psum(1, link_axis))]),
+                link_axis,
+                split_axis=0,
+                concat_axis=0,
+            ),
+            axis=2,
+        )
+
     slot_count = lax.axis_size("expert")
     step_count, row_count, _ = hidden_rows.shape
     top_count = expert_ids.shape[2]
     capacity = row_count * top_count // (slot_count - slot_count // 8) + 2
-    gathered = lax.all_gather(hidden_rows, "tensor", axis=2, tiled=True)
+    gathered = boxes_map(hidden_rows, link_axis="tensor")
     width_full = gathered.shape[2]
     plans = [
         route_plan(

time: 315 us -> 297 us (0.943)
  blocking collectives: 15.1 us -> 0 us
  local copies, waits for them, and re-layouts: 48.6 us -> 40.9 us
  starting transfers between devices: 39.8 us -> 44.2 us
    all_gather x1 -> x0, blocking collectives: 15.1 us -> none  [shards(): gathered = lax.all_gather(hidden_rows, 'tensor', axis=2, tiled=True)]
    unnamed x21 -> x18, local copies, waits for them, and re-layouts: 13.6 us -> 7.39 us
    all_to_all x0 -> x1, starting transfers between devices: none -> 4.3 us  [boxes_map(): lax.all_to_all(jnp.stack([x0 for _ in range(lax.psum(1, link_axis))]), li...]
    slice x1 -> x3, local copies, waits for them, and re-layouts: 3.46 us -> 0.18 us  [shards(): source = gathered[index]]
    all_to_all x2, waiting for transfers between devices: 69.4 us -> 66.1 us  [shards(): lax.all_to_all(partial_value, 'expert', split_axis=0, concat_axis=0, tile...]
  transfers between devices with their start and end apart: 5 -> 6, of which waited for: 5 -> 6; matrix products, arithmetic and copies ran while one was open for 12% -> 13% of each run, Pallas kernels for 0% -> 0%
where the time goes in v1:
time: 297 us; the launch traced here: 296 us
  waiting for transfers between devices  179 us (60%)
  starting transfers between devices  44.2 us (15%)
  local copies, waits for them, and re-layouts  40.9 us (14%)
  between operations  13.7 us (5%)
  matrix products  12.1 us (4%)
  other arithmetic  6.01 us (2%)
    all_to_all x2, waiting for transfers between devices, shards(): lax.all_to_all(batch, 'expert', split_axis=0, concat_axis=0, tiled=True)  78.7 us
    all_to_all x2, waiting for transfers between devices, shards(): lax.all_to_all(partial_value, 'expert', split_axis=0, concat_axis=0, tile...  66.1 us
    unnamed x2, waiting for transfers between devices  32.4 us
    all_to_all x2, starting transfers between devices, shards(): lax.all_to_all(batch, 'expert', split_axis=0, concat_axis=0, tiled=True)  24.3 us
    all_to_all x2, starting transfers between devices, shards(): lax.all_to_all(partial_value, 'expert', split_axis=0, concat_axis=0, tile...  15.4 us
    unnamed x18, local copies, waits for them, and re-layouts  7.39 us
    dot_general x2, matrix products, shards(): jnp.dot(hidden, slot_down[0], preferred_element_type=jnp.float32)  7.1 us
  transfers between devices with their start and end apart: 6, of which 6 were waited for; matrix products, arithmetic and copies ran while one was open for 13% of the time, Pallas kernels for 0%

profile of v1, /device:TPU:8, one launch (start us, length us, event | category | flops | bytes accessed | tf_op | source)
XLA Modules:
  0.0 296.2 jit_solution(4271029169418685880)
XLA Ops:
  6.5 1.6 stack.38
  8.1 4.3 %all-to-all-start = ((bf16[8,2,16,448]{3,2,1,0:T(8,128)(2,1)}), bf16[8,2,16,448]{3,2,1,0:T(8,128)(2,1)S(1)}, u32[]{:S(2)}, u32[]{:S(2)}) async-start(bf16[8,2,16,448]{3,2,1,0:T(8,128)(2,1)} %stack.38), calls=%async_computation | async-start | bytes 524288 | tf_op jit(solution)/shard_map/all_to_all | solution.py:47
  12.4 0.7 fusion.47
  13.2 0.1 squeeze.43
  13.3 0.7 fusion.46
  14.1 0.1 eq.93
  14.2 0.8 slice_bitcast_fusion.1
  14.9 0.7 pad_clamp_fusion.2
  15.6 0.7 gather_fusion
  16.2 0.7 gather_fusion.2
  17.0 0.1 and.69
  17.1 0.1 fusion.23
  17.2 0.2 reduce_window_sum.32
  17.4 0.2 select_reduce_fusion
  17.6 0.1 fusion.31
  17.7 0.1 fusion.17
  17.9 2.0 all-to-all-done
  20.0 0.2 squeeze.44
  20.2 0.7 convolution_convert_fusion.2
  20.9 1.5 reshape.207
  22.3 16.6 %all-to-all-start.3 = ((bf16[64,4,3584]{2,1,0:T(4,128)(2,1)}), bf16[64,4,3584]{2,1,0:T(4,128)(2,1)S(1)}, u32[]{:S(2)}, u32[]{:S(2)}) async-start(bf16[64,4,3584]{2,1,0:T(4,128)(2,1)} %reshape.207), calls=%async_computation.3 | async-start | bytes 3670016 | tf_op jit(solution)/shard_map/all_to_all | solution.py:84
  39.0 0.1 squeeze.37
  39.2 0.1 eq.84
  39.3 0.1 and.64
  39.5 0.1 fusion.21
  39.6 0.2 reduce_window_sum.31
  39.7 0.2 select_reduce_fusion.1
  40.1 0.1 fusion.16
  40.3 0.2 squeeze.38
  40.5 1.9 convolution_convert_fusion.3
  42.4 4.1 %reshape.202 = bf16[64,4,3584]{2,1,0:T(4,128)(2,1)} reshape(bf16[256,3584]{1,0:T(8,128)(2,1)} %convolution_convert_fusion.3) | data formatting | bytes 3670016 | tf_op jit(solution)/shard_map/reshape | solution.py:79
  46.5 38.8 %all-to-all-done.3 = bf16[64,4,3584]{2,1,0:T(4,128)(2,1)S(1)} async-done(((bf16[64,4,3584]{2,1,0:T(4,128)(2,1)}), bf16[64,4,3584]{2,1,0:T(4,128)(2,1)S(1)}, u32[]{:S(2)}, u32[]{:S(2)}) %all-to-all-start.3) | async-done | bytes 1835040 | tf_op jit(solution)/shard_map/all_to_all | solution.py:84
  85.3 7.7 %all-to-all-start.1 = ((bf16[64,4,3584]{2,1,0:T(4,128)(2,1)}), bf16[64,4,3584]{2,1,0:T(4,128)(2,1)}, u32[]{:S(2)}, u32[]{:S(2)}) async-start(bf16[64,4,3584]{2,1,0:T(4,128)(2,1)} %reshape.202), calls=%async_computation.1 | async-start | bytes 3670016 | tf_op jit(solution)/shard_map/all_to_all | solution.py:84
  93.0 1.5 reshape.208
  94.5 2.9 convolution_convert_fusion
  97.4 1.5 reshape.209
  98.9 39.9 %all-to-all-done.1 = bf16[64,4,3584]{2,1,0:T(4,128)(2,1)} async-done(((bf16[64,4,3584]{2,1,0:T(4,128)(2,1)}), bf16[64,4,3584]{2,1,0:T(4,128)(2,1)}, u32[]{:S(2)}, u32[]{:S(2)}) %all-to-all-start.1) | async-done | bytes 1835040 | tf_op jit(solution)/shard_map/all_to_all | solution.py:84
  138.7 7.6 %all-to-all-start.4 = ((bf16[64,4,3584]{2,1,0:T(4,128)(2,1)}), bf16[64,4,3584]{2,1,0:T(4,128)(2,1)S(1)}, u32[]{:S(2)}, u32[]{:S(2)}) async-start(bf16[64,4,3584]{2,1,0:T(4,128)(2,1)} %reshape.209), calls=%async_computation.4 | async-start | bytes 3670016 | tf_op jit(solution)/shard_map/all_to_all | solution.py:93
  146.4 3.9 %reshape.203 = bf16[256,3584]{1,0:T(8,128)(2,1)} reshape(bf16[64,4,3584]{2,1,0:T(4,128)(2,1)} %all-to-all-done.1) | data formatting | bytes 3670016 | tf_op jit(solution)/shard_map/reshape | solution.py:85
  150.3 4.2 %convolution_convert_fusion.1 = bf16[256,3584]{1,0:T(8,128)(2,1)} fusion(bf16[1,128,3584]{2,1,0:T(8,128)(2,1)S(1)} %copy-done, bf16[256,3584]{1,0:T(8,128)(2,1)} %reshape.203, bf16[1,3584,128]{2,1,0:T(8,128)(2,1)} %param.22), kind=kOutput, calls=%fused_computation.5 | convolution fusion | flops 470843392 | bytes 5505024 | tf_op jit(solution)/shard_map/dot_general | solution.py:89
  154.5 4.1 %reshape.204 = bf16[64,4,3584]{2,1,0:T(4,128)(2,1)} reshape(bf16[256,3584]{1,0:T(8,128)(2,1)} %convolution_convert_fusion.1) | data formatting | bytes 3670016 | tf_op jit(solution)/shard_map/reshape | solution.py:92
  158.5 31.5 %all-to-all-done.4 = bf16[64,4,3584]{2,1,0:T(4,128)(2,1)S(1)} async-done(((bf16[64,4,3584]{2,1,0:T(4,128)(2,1)}), bf16[64,4,3584]{2,1,0:T(4,128)(2,1)S(1)}, u32[]{:S(2)}, u32[]{:S(2)}) %all-to-all-start.4) | async-done | bytes 1835040 | tf_op jit(solution)/shard_map/all_to_all | solution.py:93
  190.1 1.3 copy-done.1
  191.3 7.8 %all-to-all-start.2 = ((bf16[64,4,3584]{2,1,0:T(4,128)(2,1)}), bf16[64,4,3584]{2,1,0:T(4,128)(2,1)}, u32[]{:S(2)}, u32[]{:S(2)}) async-start(bf16[64,4,3584]{2,1,0:T(4,128)(2,1)} %reshape.204), calls=%async_computation.2 | async-start | bytes 3670016 | tf_op jit(solution)/shard_map/all_to_all | solution.py:93
  199.1 0.2 reduce-scatter.4.cloned.1.call-start
  199.4 0.1 squeeze.45
  199.6 0.1 mul.98
  199.8 0.1 squeeze.41
  199.9 0.1 mul.89
  200.1 1.9 convolution_bitcast_fusion
  202.0 0.5 convolution_bitcast_fusion.1
  202.5 3.0 reshape.210
  205.5 2.0 gather_fusion.3
  207.5 34.6 %all-to-all-done.2 = bf16[64,4,3584]{2,1,0:T(4,128)(2,1)} async-done(((bf16[64,4,3584]{2,1,0:T(4,128)(2,1)}), bf16[64,4,3584]{2,1,0:T(4,128)(2,1)}, u32[]{:S(2)}, u32[]{:S(2)}) %all-to-all-start.2) | async-done | bytes 1835040 | tf_op jit(solution)/shard_map/all_to_all | solution.py:93
  242.1 2.9 reshape.205
  245.1 2.0 gather_fusion.1
  247.1 1.9 bitcast_reduce_fusion
  249.0 1.9 bitcast_reduce_fusion.1
  251.0 0.1 fusion.7
  251.1 2.4 copy.56
  253.5 1.6 reshape.254
  255.2 32.4 %reduce-scatter.4.cloned.1.call-done = bf16[448,32]{1,0:T(8,128)(2,1)} async-done(((bf16[3584,32]{1,0:T(8,128)(2,1)}), bf16[448,32]{1,0:T(8,128)(2,1)}) %reduce-scatter.4.cloned.1.call-update) | async-done | bytes 28688
  287.5 1.0 reshape.255
  288.6 0.7 copy.57
  (39 shorter events, 1.3 us)
Async XLA Ops:
  6.5 87.9 %copy-start = (bf16[1,128,3584]{2,1,0:T(8,128)(2,1)S(1)}, bf16[1,128,3584]{2,1,0:T(8,128)(2,1)}, u32[]{:S(2)}) copy-start(bf16[1,128,3584]{2,1,0:T(8,128)(2,1)} %param.23) | copy-start | bytes 2752516
  8.1 11.8 %all-to-all-start = ((bf16[8,2,16,448]{3,2,1,0:T(8,128)(2,1)}), bf16[8,2,16,448]{3,2,1,0:T(8,128)(2,1)S(1)}, u32[]{:S(2)}, u32[]{:S(2)}) async-start(bf16[8,2,16,448]{3,2,1,0:T(8,128)(2,1)} %stack.38), calls=%async_computation | async-start | bytes 524288 | tf_op jit(solution)/shard_map/all_to_all | solution.py:47
  22.3 62.9 %all-to-all-start.3 = ((bf16[64,4,3584]{2,1,0:T(4,128)(2,1)}), bf16[64,4,3584]{2,1,0:T(4,128)(2,1)S(1)}, u32[]{:S(2)}, u32[]{:S(2)}) async-start(bf16[64,4,3584]{2,1,0:T(4,128)(2,1)} %reshape.207), calls=%async_computation.3 | async-start | bytes 3670016 | tf_op jit(solution)/shard_map/all_to_all | solution.py:84
  85.3 53.5 %all-to-all-start.1 = ((bf16[64,4,3584]{2,1,0:T(4,128)(2,1)}), bf16[64,4,3584]{2,1,0:T(4,128)(2,1)}, u32[]{:S(2)}, u32[]{:S(2)}) async-start(bf16[64,4,3584]{2,1,0:T(4,128)(2,1)} %reshape.202), calls=%async_computation.1 | async-start | bytes 3670016 | tf_op jit(solution)/shard_map/all_to_all | solution.py:84
  138.7 51.3 %all-to-all-start.4 = ((bf16[64,4,3584]{2,1,0:T(4,128)(2,1)}), bf16[64,4,3584]{2,1,0:T(4,128)(2,1)S(1)}, u32[]{:S(2)}, u32[]{:S(2)}) async-start(bf16[64,4,3584]{2,1,0:T(4,128)(2,1)} %reshape.209), calls=%async_computation.4 | async-start | bytes 3670016 | tf_op jit(solution)/shard_map/all_to_all | solution.py:93
  158.5 40.8 %copy-start.4 = (f32[2,16,8]{1,2,0:T(8,128)S(1)}, f32[2,16,8]{1,2,0:T(8,128)}, u32[]{:S(2)}) copy-start(f32[2,16,8]{1,2,0:T(8,128)} %param.21) | copy-start | bytes 3076
  190.0 1.3 copy-start.1
  191.3 50.8 %all-to-all-start.2 = ((bf16[64,4,3584]{2,1,0:T(4,128)(2,1)}), bf16[64,4,3584]{2,1,0:T(4,128)(2,1)}, u32[]{:S(2)}, u32[]{:S(2)}) async-start(bf16[64,4,3584]{2,1,0:T(4,128)(2,1)} %reshape.204), calls=%async_computation.2 | async-start | bytes 3670016 | tf_op jit(solution)/shard_map/all_to_all | solution.py:93
  199.1 3.0 copy-start.2
  199.1 2.9 copy-start.3
  199.1 88.4 %reduce-scatter.4.cloned.1.call-start = ((), (), s32[]{:S(2)}) async-start(), calls=%async_computation.6 | async-start | bytes 1032192
Sparse Core Ops, SparseCore 0:
  255.3 32.2 reduce-scatter.3
